TPU v7x, 512 devices: a whole 4x8x8 slice. The times are simulated.
512 devices in a mesh: tm: 32 (over y, x), rows: 16 (over z, core).
Axes of the slice: x: 4, y: 8, z: 8, core: 2. Of those that a mesh axis runs over, the one named last changes fastest.
Arguments:
- features: bfloat16 [64, 16, 40, 384], P('tm', 'rows'), may hold values from -6 to 6
- gain_one: float32 [384], replicated, may hold values from 0.1 to 1.9
- weight_one: bfloat16 [384, 3, 3, 3, 384], P('rows'), may hold values from -0.0625 to 0.0625
- bias_one: float32 [384], replicated, may hold values from -3 to 3
- gain_two: float32 [384], replicated, may hold values from 0.1 to 1.9
- weight_two: bfloat16 [384, 3, 3, 3, 384], P('rows'), may hold values from -0.0625 to 0.0625
- bias_two: float32 [384], replicated, may hold values from -3 to 3
Outputs:
- block_out: bfloat16 [64, 16, 40, 384], P('tm', 'rows')
All inputs are finite; a program needn't handle non-finite values.
Results may differ from a plain program's by a relative error of at most 0.0049.
Values may be sent and summed in bfloat16 or wider, within the bound.
No kernel may reach another device: no remote copies, remote signals or barrier semaphores. Data moves between devices by JAX's collectives and lax.ppermute only.
A program may use at most 64 MiB of HBM per device.

v0:
```python
import jax
import jax.numpy as jnp
from jax import lax
from jax.sharding import PartitionSpec as P


def passed_along(x, axis, by):
    peers = lax.axis_size(axis)
    pairs = [(i, i + by) for i in range(peers) if 0 <= i + by < peers]
    return lax.ppermute(x, axis, pairs)


def norm_silu(values, norm_gain):
    values = values.astype(jnp.float32)
    mean_square = jnp.mean(values * values, axis=-1, keepdims=True)
    scaled = values * lax.rsqrt(mean_square + 1e-06) * norm_gain
    return jax.nn.silu(scaled).astype(jnp.bfloat16)


def causal_conv(extended, kernel, bias_part):
    frames = extended.shape[0] - 2
    height = extended.shape[1]
    columns = extended.shape[2]
    channels = extended.shape[3]
    part_width = kernel.shape[0]
    folded = 9 * part_width
    padded_width = (folded + 127) // 128 * 128
    padded = jnp.pad(extended, ((0, 0), (1, 1), (1, 1), (0, 0)))
    summed = jnp.zeros((frames, height, columns, part_width), jnp.float32)
    for tap_time in range(3):
        slab = padded[tap_time : tap_time + frames]
        taps = jnp.transpose(kernel[:, tap_time], (1, 2, 0, 3)).reshape(folded, channels)
        taps = jnp.pad(taps, ((0, padded_width - folded), (0, 0)))
        product = lax.dot_general(
            slab.reshape(-1, channels),
            taps,
            (((1,), (1,)), ((), ())),
            preferred_element_type=jnp.float32,
        )
        product = product[:, :folded].reshape(frames, height + 2, columns + 2, 3, 3, part_width)
        for tap_row in range(3):
            for tap_col in range(3):
                summed = (
                    summed
                    + product[
                        :, tap_row : tap_row + height, tap_col : tap_col + columns, tap_row, tap_col
                    ]
                )
    return summed + bias_part


def shards(features, gain_one, weight_one, bias_one, gain_two, weight_two, bias_two):
    part_width = weight_one.shape[0]
    offset = lax.axis_index("rows") * part_width
    bias_first = lax.dynamic_slice_in_dim(bias_one, offset, part_width, 0)
    bias_second = lax.dynamic_slice_in_dim(bias_two, offset, part_width, 0)
    normed_one = norm_silu(features, gain_one)
    prior_one = passed_along(normed_one, "tm", 1)
    extended_one = jnp.concatenate([prior_one, normed_one], 0)
    full_one = lax.all_gather(extended_one, "rows", axis=1, tiled=True)
    conv_one = causal_conv(full_one, weight_one, bias_first).astype(jnp.bfloat16)
    own_rows = lax.all_to_all(conv_one, "rows", split_axis=1, concat_axis=3, tiled=True)
    normed_two = norm_silu(own_rows, gain_two)
    prior_two = passed_along(normed_two, "tm", 1)
    extended_two = jnp.concatenate([prior_two, normed_two], 0)
    full_two = lax.all_gather(extended_two, "rows", axis=1, tiled=True)
    conv_two = causal_conv(full_two, weight_two, bias_second)
    returned = lax.all_to_all(conv_two, "rows", split_axis=1, concat_axis=3, tiled=True)
    return (features.astype(jnp.float32) + returned).astype(jnp.bfloat16)


def solution(mesh):
    in_specs = (
        P("tm", "rows", None, None),
        P(),
        P("rows", None, None, None, None),
        P(),
        P(),
        P("rows", None, None, None, None),
        P(),
    )
    out_specs = P("tm", "rows", None, None)
    return jax.shard_map(shards, mesh=mesh, in_specs=in_specs, out_specs=out_specs, check_vma=False)
```

profile of v0, /device:TPU:1, one launch (start us, length us, event | category | flops | bytes accessed | tf_op | source)
XLA Modules:
  0.0 217.8 jit_solution(14636832090744077345)
XLA Ops:
  6.5 0.9 fusion.25
  7.5 0.9 fusion.32
  8.4 3.9 %collective-permute-start = (bf16[2,1,40,384]{3,2,1,0:T(8,128)(2,1)S(1)}, bf16[2,1,40,384]{3,2,1,0:T(8,128)(2,1)S(1)}, u32[]{:S(2)}, u32[]{:S(2)}) collective-permute-start(bf16[2,1,40,384]{3,2,1,0:T(8,128)(2,1)S(1)} %fusion.32), channel_id=1, source_target_pairs={{0,16},{16,32},{32,48},{48,64},{64,80},{80,96},{96,112},{112,128},... | collective-permute-start | bytes 184328 | tf_op jit(solution)/shard_map/ppermute | solution.py:10
  12.4 1.3 collective-permute-done
  13.7 0.7 maximum_bitcast_fusion
  14.3 0.0 all-gather.3.cloned.1.call-update
  14.3 0.0 all-gather.5.cloned.1.call-start
  14.4 0.8 dynamic_slice.6
  15.2 1.1 fusion.35
  16.3 48.9 %all-gather.3.cloned.1.call-done = bf16[4,16,40,384]{3,2,0,1:T(8,128)(2,1)} async-done(((bf16[4,1,40,384]{3,2,0,1:T(8,128)(2,1)}), bf16[4,16,40,384]{3,2,0,1:T(8,128)(2,1)}) %all-gather.3.cloned.1.call-update) | async-done | bytes 1966096 | tf_op jit(solution)/shard_map/all_gather | solution.py:60
  65.2 4.8 %pad_slice_fusion.5 = (bf16[2,18,42,384]{3,2,0,1:T(8,128)(2,1)S(1)}, bf16[2,18,42,384]{3,2,0,1:T(8,128)(2,1)}, bf16[2,18,42,384]{3,2,0,1:T(8,128)(2,1)S(1)}) fusion(bf16[4,16,40,384]{3,2,0,1:T(8,128)(2,1)} %all-gather.3.cloned.1.call-done), kind=kLoop, calls=%fused_computation.5 | loop fusion | bytes 5449728 | tf_op jit(solution)/shard_map/slice | solution.py:31
  70.0 0.1 copy.59
  70.2 1.3 reshape.154
  71.5 1.9 fusion.38
  73.4 4.3 %reshape.156 = f32[2,18,42,3,3,24]{2,1,0,5,4,3:T(8,128)} reshape(f32[1512,216]{0,1:T(8,128)S(1)} %fusion.38) | data formatting | bytes 2612736 | tf_op jit(solution)/shard_map/reshape | solution.py:40
  77.7 1.5 copy.58
  79.2 1.4 reshape.151
  80.5 1.9 fusion.37
  82.4 4.4 %reshape.153 = f32[2,18,42,3,3,24]{2,1,0,5,4,3:T(8,128)} reshape(f32[1512,216]{0,1:T(8,128)S(1)} %fusion.37) | data formatting | bytes 2612736 | tf_op jit(solution)/shard_map/reshape | solution.py:40
  86.8 0.1 copy.57
  86.9 0.3 reshape.148
  87.3 0.6 fusion.36
  87.9 4.3 %reshape.150 = f32[2,18,42,3,3,24]{2,1,0,5,4,3:T(8,128)} reshape(f32[1512,216]{0,1:T(8,128)S(1)} %fusion.36) | data formatting | bytes 2612736 | tf_op jit(solution)/shard_map/reshape | solution.py:40
  92.2 7.0 %fusion.14 = bf16[2,16,40,24]{2,1,0,3:T(8,128)(2,1)S(1)} fusion(f32[2,18,42,3,3,24]{2,1,0,5,4,3:T(8,128)} %reshape.156, f32[2,18,42,3,3,24]{2,1,0,5,4,3:T(8,128)} %reshape.153, f32[2,18,42,3,3,24]{2,1,0,5,4,3:T(8,128)} %reshape.150, f32[24]{0:T(128)S(1)} %dynamic_slice.6), kind=kLoop, calls=%fused_computation.47 | loop fusion | flops 860160 | bytes 3379296 | tf_op jit(solution)/shard_map/convert_element_type | solution.py:61
  99.2 0.0 copy-start.2
  99.2 0.2 copy.77
  99.3 0.0 copy-start.1
  99.3 0.2 reshape.192
  99.6 12.0 %all_to_all.27 = bf16[16,2,960]{2,1,0:T(2,128)(2,1)S(1)} all-to-all(bf16[16,2,960]{2,1,0:T(2,128)(2,1)S(1)} %reshape.192), channel_id=1, replica_groups=mesh['tm'=32,'rows'=16] {'rows'}, dimensions={0} | all-to-all | bytes 122880 | tf_op jit(solution)/shard_map/all_to_all | solution.py:62
  111.6 0.2 reshape.193
  111.8 0.1 bitcast_convert_fusion
  112.0 0.4 multiply_reduce_fusion
  112.4 0.1 copy.62
  112.6 0.1 multiply_convert_fusion
  112.7 3.3 %collective-permute-start.1 = (bf16[2,1,40,384]{3,2,1,0:T(8,128)(2,1)S(1)}, bf16[2,1,40,384]{3,2,1,0:T(8,128)(2,1)S(1)}, u32[]{:S(2)}, u32[]{:S(2)}) collective-permute-start(bf16[2,1,40,384]{3,2,1,0:T(8,128)(2,1)S(1)} %multiply_convert_fusion), channel_id=1, source_target_pairs={{0,16},{16,32},{32,48},{48,64},{64,80},{80,96},{96,112},{112,128},... | collective-permute-start | bytes 184328 | tf_op jit(solution)/shard_map/ppermute | solution.py:10
  116.0 1.1 collective-permute-done.1
  117.1 0.7 maximum_bitcast_fusion.1
  117.7 0.0 all-gather.5.cloned.1.call-update
  117.8 0.8 dynamic_slice.7
  118.5 0.1 fusion.34
  118.6 41.3 %all-gather.5.cloned.1.call-done = bf16[4,16,40,384]{3,2,0,1:T(8,128)(2,1)} async-done(((bf16[4,1,40,384]{3,2,0,1:T(8,128)(2,1)}), bf16[4,16,40,384]{3,2,0,1:T(8,128)(2,1)}) %all-gather.5.cloned.1.call-update) | async-done | bytes 1966096 | tf_op jit(solution)/shard_map/all_gather | solution.py:66
  159.9 4.8 %pad_slice_fusion.2 = (bf16[2,18,42,384]{3,2,0,1:T(8,128)(2,1)S(1)}, bf16[2,18,42,384]{3,2,0,1:T(8,128)(2,1)}, bf16[2,18,42,384]{3,2,0,1:T(8,128)(2,1)S(1)}) fusion(bf16[4,16,40,384]{3,2,0,1:T(8,128)(2,1)} %all-gather.5.cloned.1.call-done), kind=kLoop, calls=%fused_computation.2 | loop fusion | bytes 5449728 | tf_op jit(solution)/shard_map/slice | solution.py:31
  164.7 0.1 copy.66
  164.8 1.3 reshape.163
  166.1 1.9 fusion.41
  168.0 4.3 %reshape.165 = f32[2,18,42,3,3,24]{2,1,0,5,4,3:T(8,128)} reshape(f32[1512,216]{0,1:T(8,128)S(1)} %fusion.41) | data formatting | bytes 2612736 | tf_op jit(solution)/shard_map/reshape | solution.py:40
  172.4 1.5 copy.65
  173.8 1.4 reshape.160
  175.2 1.9 fusion.40
  177.1 4.4 %reshape.162 = f32[2,18,42,3,3,24]{2,1,0,5,4,3:T(8,128)} reshape(f32[1512,216]{0,1:T(8,128)S(1)} %fusion.40) | data formatting | bytes 2612736 | tf_op jit(solution)/shard_map/reshape | solution.py:40
  181.5 0.1 copy.64
  181.6 0.3 reshape.157
  181.9 0.6 fusion.39
  182.5 4.3 %reshape.159 = f32[2,18,42,3,3,24]{2,1,0,5,4,3:T(8,128)} reshape(f32[1512,216]{0,1:T(8,128)S(1)} %fusion.39) | data formatting | bytes 2612736 | tf_op jit(solution)/shard_map/reshape | solution.py:40
  186.8 7.0 %fusion.1 = f32[2,16,40,24]{2,1,0,3:T(8,128)S(1)} fusion(f32[2,18,42,3,3,24]{2,1,0,5,4,3:T(8,128)} %reshape.165, f32[2,18,42,3,3,24]{2,1,0,5,4,3:T(8,128)} %reshape.162, f32[2,18,42,3,3,24]{2,1,0,5,4,3:T(8,128)} %reshape.159, f32[24]{0:T(128)S(1)} %dynamic_slice.7), kind=kLoop, calls=%fused_computation.8 | loop fusion | flops 829440 | bytes 3440736 | tf_op jit(solution)/shard_map/add | solution.py:49
  193.8 0.0 copy-start
  193.8 0.2 copy.76
  194.0 0.7 reshape.194
  194.8 13.2 %all_to_all.28 = f32[16,1,1920]{2,1,0:T(1,128)S(1)} all-to-all(f32[16,1,1920]{2,1,0:T(1,128)S(1)} %reshape.194), channel_id=1, replica_groups=mesh['tm'=32,'rows'=16] {'rows'}, dimensions={0} | all-to-all | bytes 245760 | tf_op jit(solution)/shard_map/all_to_all | solution.py:68
  208.0 0.5 broadcast.93
  208.5 0.9 reduce.5
  209.4 0.7 reshape.195
  210.1 0.1 copy.69
  210.3 0.6 fusion.33
  (6 shorter events, 0.0 us)
Async XLA Ops:
  6.5 58.7 %all-gather.3.cloned.1.call-start = ((), (), s32[]{:S(2)}) async-start(), calls=%async_computation.2 | async-start | bytes 2088960 | tf_op jit(solution)/shard_map/all_gather | solution.py:60
  8.4 5.2 %collective-permute-start = (bf16[2,1,40,384]{3,2,1,0:T(8,128)(2,1)S(1)}, bf16[2,1,40,384]{3,2,1,0:T(8,128)(2,1)S(1)}, u32[]{:S(2)}, u32[]{:S(2)}) collective-permute-start(bf16[2,1,40,384]{3,2,1,0:T(8,128)(2,1)S(1)} %fusion.32), channel_id=1, source_target_pairs={{0,16},{16,32},{32,48},{48,64},{64,80},{80,96},{96,112},{112,128},... | collective-permute-start | bytes 184328 | tf_op jit(solution)/shard_map/ppermute | solution.py:10
  14.3 145.5 %all-gather.5.cloned.1.call-start = ((), (), s32[]{:S(2)}) async-start(), calls=%async_computation.3 | async-start | bytes 2088960 | tf_op jit(solution)/shard_map/all_gather | solution.py:66
  99.2 13.4 %copy-start.2 = (f32[384]{0:T(512)S(1)}, f32[384]{0:T(512)}, u32[]{:S(2)}) copy-start(f32[384]{0:T(512)} %param.11) | copy-start | bytes 4612
  99.3 19.2 %copy-start.1 = (bf16[24,3,3,3,384]{4,0,3,2,1:T(8,128)(2,1)S(1)}, bf16[24,3,3,3,384]{4,0,3,2,1:T(8,128)(2,1)}, u32[]{:S(2)}) copy-start(bf16[24,3,3,3,384]{4,0,3,2,1:T(8,128)(2,1)} %param.12) | copy-start | bytes 1492996
  112.7 4.4 %collective-permute-start.1 = (bf16[2,1,40,384]{3,2,1,0:T(8,128)(2,1)S(1)}, bf16[2,1,40,384]{3,2,1,0:T(8,128)(2,1)S(1)}, u32[]{:S(2)}, u32[]{:S(2)}) collective-permute-start(bf16[2,1,40,384]{3,2,1,0:T(8,128)(2,1)S(1)} %multiply_convert_fusion), channel_id=1, source_target_pairs={{0,16},{16,32},{32,48},{48,64},{64,80},{80,96},{96,112},{112,128},... | collective-permute-start | bytes 184328 | tf_op jit(solution)/shard_map/ppermute | solution.py:10
  193.8 16.5 %copy-start = (bf16[2,1,40,384]{3,2,1,0:T(8,128)(2,1)S(1)}, bf16[2,1,40,384]{3,2,1,0:T(8,128)(2,1)}, u32[]{:S(2)}) copy-start(bf16[2,1,40,384]{3,2,1,0:T(8,128)(2,1)} %param.7) | copy-start | bytes 184324
Sparse Core Ops, SparseCore 0:
  14.5 50.7 all-gather.2
  117.9 41.9 all-gather.4
where the time goes:
time: 218 us
  waiting for transfers between devices  92.6 us (42%)
  local copies, waits for them, and re-layouts  50.8 us (23%)
  blocking collectives  25.2 us (12%)
  other arithmetic  19.4 us (9%)
  between operations  13.6 us (6%)
  matrix products  8.8 us (4%)
  starting transfers between devices  7.28 us (3%)
    all_gather x1, waiting for transfers between devices, shards(): full_one = lax.all_gather(extended_one, 'rows', axis=1, tiled=True)  48.9 us
    all_gather x1, waiting for transfers between devices, shards(): full_two = lax.all_gather(extended_two, 'rows', axis=1, tiled=True)  41.3 us
    reshape x6, local copies, waits for them, and re-layouts, causal_conv(): product[:, :folded]  25.9 us
    all_to_all x1, blocking collectives, shards(): lax.all_to_all(conv_two, 'rows', split_axis=1, concat_axis=3, tiled=True)  13.2 us
    slice x8, local copies, waits for them, and re-layouts, causal_conv(): slab = padded[tap_time:tap_time + frames]  13.1 us
    all_to_all x1, blocking collectives, shards(): lax.all_to_all(conv_one, 'rows', split_axis=1, concat_axis=3, tiled=True)  12 us
    dot_general x6, matrix products, causal_conv(): lax.dot_general(slab.reshape(-1, channels), taps, (((1,), (1,)), ((), ())...  8.8 us
    ppermute x2, starting transfers between devices, passed_along(): return lax.ppermute(x, axis, pairs)  7.24 us
  transfers between devices with their start and end apart: 4, of which 4 were waited for; matrix products, arithmetic and copies ran while one was open for 1% of the time, Pallas kernels for 0%

commit v1 on v0

--- a/solution.py
+++ b/solution.py
@@ -57,7 +57,12 @@
     normed_one = norm_silu(features, gain_one)
     prior_one = passed_along(normed_one, "tm", 1)
     extended_one = jnp.concatenate([prior_one, normed_one], 0)
-    full_one = lax.all_gather(extended_one, "rows", axis=1, tiled=True)
+    ring = [extended_one]
+    for hop in range(15):
+        ring.append(lax.ppermute(ring[-1], "rows", [(dev, (dev + 1) % 16) for dev in range(16)]))
+    full_one = jnp.roll(
+        jnp.concatenate(ring[::-1], axis=1), (lax.axis_index("rows") + 1) * ring[0].shape[1], axis=1
+    )
     conv_one = causal_conv(full_one, weight_one, bias_first).astype(jnp.bfloat16)
     own_rows = lax.all_to_all(conv_one, "rows", split_axis=1, concat_axis=3, tiled=True)
     normed_two = norm_silu(own_rows, gain_two)

time: 218 us -> 263 us (1.21)
  waiting for transfers between devices: 92.6 us -> 124 us
  starting transfers between devices: 7.28 us -> 13.9 us
  blocking collectives: 25.2 us -> 31.1 us
    ppermute x0 -> x15, waiting for transfers between devices: none -> 76.6 us  [shards(): lax.ppermute(ring[-1], 'rows', [(dev, (dev + 1) % 16) for dev in range(16)])]
    all_gather x1 -> x0, waiting for transfers between devices: 48.9 us -> none  [shards(): full_one = lax.all_gather(extended_one, 'rows', axis=1, tiled=True)]
    all_to_all x1, blocking collectives: 12 us -> 17.9 us  [shards(): lax.all_to_all(conv_one, 'rows', split_axis=1, concat_axis=3, tiled=True)]
    ppermute x0 -> x15, starting transfers between devices: none -> 5.74 us  [shards(): lax.ppermute(ring[-1], 'rows', [(dev, (dev + 1) % 16) for dev in range(16)])]
    slice x8 -> x5, local copies, waits for them, and re-layouts: 13.1 us -> 8.86 us  [causal_conv(): slab = padded[tap_time:tap_time + frames]]
    all_gather x1, waiting for transfers between devices: 41.3 us -> 44.9 us  [shards(): full_two = lax.all_gather(extended_two, 'rows', axis=1, tiled=True)]
  transfers between devices with their start and end apart: 4 -> 18, of which waited for: 4 -> 18; matrix products, arithmetic and copies ran while one was open for 1% -> 1% of each run, Pallas kernels for 0% -> 0%
where the time goes in v1:
time: 263 us; the launch traced here: 262 us
  waiting for transfers between devices  124 us (47%)
  local copies, waits for them, and re-layouts  50.2 us (19%)
  blocking collectives  31.1 us (12%)
  other arithmetic  18.9 us (7%)
  starting transfers between devices  13.9 us (5%)
  between operations  13.9 us (5%)
  matrix products  10.1 us (4%)
    ppermute x15, waiting for transfers between devices, shards(): lax.ppermute(ring[-1], 'rows', [(dev, (dev + 1) % 16) for dev in range(16)])  76.6 us
    all_gather x1, waiting for transfers between devices, shards(): full_two = lax.all_gather(extended_two, 'rows', axis=1, tiled=True)  44.9 us
    reshape x6, local copies, waits for them, and re-layouts, causal_conv(): product[:, :folded]  26.1 us
    all_to_all x1, blocking collectives, shards(): lax.all_to_all(conv_one, 'rows', split_axis=1, concat_axis=3, tiled=True)  17.9 us
    all_to_all x1, blocking collectives, shards(): lax.all_to_all(conv_two, 'rows', split_axis=1, concat_axis=3, tiled=True)  13.2 us
    dot_general x6, matrix products, causal_conv(): lax.dot_general(slab.reshape(-1, channels), taps, (((1,), (1,)), ((), ())...  10.1 us
    slice x5, local copies, waits for them, and re-layouts, causal_conv(): slab = padded[tap_time:tap_time + frames]  8.86 us
    reshape x6, local copies, waits for them, and re-layouts, causal_conv(): slab.reshape(-1, channels)  8.65 us
  transfers between devices with their start and end apart: 18, of which 18 were waited for; matrix products, arithmetic and copies ran while one was open for 1% of the time, Pallas kernels for 0%

profile of v1, /device:TPU:1, one launch (start us, length us, event | category | flops | bytes accessed | tf_op | source)
XLA Modules:
  0.0 261.9 jit_solution(17799050292261665568)
XLA Ops:
  6.5 0.9 fusion.25
  7.5 0.9 fusion.32
  8.4 3.9 %collective-permute-start = (bf16[2,1,40,384]{3,2,1,0:T(8,128)(2,1)S(1)}, bf16[2,1,40,384]{3,2,1,0:T(8,128)(2,1)S(1)}, u32[]{:S(2)}, u32[]{:S(2)}) collective-permute-start(bf16[2,1,40,384]{3,2,1,0:T(8,128)(2,1)S(1)} %fusion.32), channel_id=1, source_target_pairs={{0,16},{16,32},{32,48},{48,64},{64,80},{80,96},{96,112},{112,128},... | collective-permute-start | bytes 184328 | tf_op jit(solution)/shard_map/ppermute | solution.py:10
  12.4 1.3 collective-permute-done
  13.7 3.5 %collective-permute-start.1 = (bf16[4,1,40,384]{3,2,1,0:T(8,128)(2,1)S(1)}, bf16[4,1,40,384]{3,2,1,0:T(8,128)(2,1)S(1)}, u32[]{:S(2)}, u32[]{:S(2)}) collective-permute-start(bf16[4,1,40,384]{3,2,1,0:T(8,128)(2,1)S(1)} %pad_maximum_fusion), channel_id=1, source_target_pairs={{0,1},{1,2},{2,3},{3,4},{4,5},{5,6},{6,7},{7,8},{8,9},{9,10},{10,1... | collective-permute-start | bytes 368648 | tf_op jit(solution)/shard_map/ppermute | solution.py:62
  17.2 2.1 collective-permute-done.1
  19.3 2.2 collective-permute-start.2
  21.5 4.7 %collective-permute-done.2 = bf16[4,1,40,384]{3,2,1,0:T(8,128)(2,1)S(1)} collective-permute-done((bf16[4,1,40,384]{3,2,1,0:T(8,128)(2,1)S(1)}, bf16[4,1,40,384]{3,2,1,0:T(8,128)(2,1)S(1)}, u32[]{:S(2)}, u32[]{:S(2)}) %collective-permute-start.2) | collective-permute-done | bytes 122912 | tf_op jit(solution)/shard_map/ppermute | solution.py:62
  26.2 5.5 %collective-permute-done.3 = bf16[4,1,40,384]{3,2,1,0:T(8,128)(2,1)S(1)} collective-permute-done((bf16[4,1,40,384]{3,2,1,0:T(8,128)(2,1)S(1)}, bf16[4,1,40,384]{3,2,1,0:T(8,128)(2,1)S(1)}, u32[]{:S(2)}, u32[]{:S(2)}) %collective-permute-start.3) | collective-permute-done | bytes 122912 | tf_op jit(solution)/shard_map/ppermute | solution.py:62
  31.8 5.5 %collective-permute-done.4 = bf16[4,1,40,384]{3,2,1,0:T(8,128)(2,1)S(1)} collective-permute-done((bf16[4,1,40,384]{3,2,1,0:T(8,128)(2,1)S(1)}, bf16[4,1,40,384]{3,2,1,0:T(8,128)(2,1)S(1)}, u32[]{:S(2)}, u32[]{:S(2)}) %collective-permute-start.4) | collective-permute-done | bytes 122912 | tf_op jit(solution)/shard_map/ppermute | solution.py:62
  37.3 5.5 %collective-permute-done.5 = bf16[4,1,40,384]{3,2,1,0:T(8,128)(2,1)S(1)} collective-permute-done((bf16[4,1,40,384]{3,2,1,0:T(8,128)(2,1)S(1)}, bf16[4,1,40,384]{3,2,1,0:T(8,128)(2,1)S(1)}, u32[]{:S(2)}, u32[]{:S(2)}) %collective-permute-start.5) | collective-permute-done | bytes 122912 | tf_op jit(solution)/shard_map/ppermute | solution.py:62
  42.8 5.5 %collective-permute-done.6 = bf16[4,1,40,384]{3,2,1,0:T(8,128)(2,1)S(1)} collective-permute-done((bf16[4,1,40,384]{3,2,1,0:T(8,128)(2,1)S(1)}, bf16[4,1,40,384]{3,2,1,0:T(8,128)(2,1)S(1)}, u32[]{:S(2)}, u32[]{:S(2)}) %collective-permute-start.6) | collective-permute-done | bytes 122912 | tf_op jit(solution)/shard_map/ppermute | solution.py:62
  48.3 5.5 %collective-permute-done.7 = bf16[4,1,40,384]{3,2,1,0:T(8,128)(2,1)S(1)} collective-permute-done((bf16[4,1,40,384]{3,2,1,0:T(8,128)(2,1)S(1)}, bf16[4,1,40,384]{3,2,1,0:T(8,128)(2,1)S(1)}, u32[]{:S(2)}, u32[]{:S(2)}) %collective-permute-start.7) | collective-permute-done | bytes 122912 | tf_op jit(solution)/shard_map/ppermute | solution.py:62
  53.8 5.5 %collective-permute-done.8 = bf16[4,1,40,384]{3,2,1,0:T(8,128)(2,1)S(1)} collective-permute-done((bf16[4,1,40,384]{3,2,1,0:T(8,128)(2,1)S(1)}, bf16[4,1,40,384]{3,2,1,0:T(8,128)(2,1)S(1)}, u32[]{:S(2)}, u32[]{:S(2)}) %collective-permute-start.8) | collective-permute-done | bytes 122912 | tf_op jit(solution)/shard_map/ppermute | solution.py:62
  59.3 5.5 %collective-permute-done.9 = bf16[4,1,40,384]{3,2,1,0:T(8,128)(2,1)S(1)} collective-permute-done((bf16[4,1,40,384]{3,2,1,0:T(8,128)(2,1)S(1)}, bf16[4,1,40,384]{3,2,1,0:T(8,128)(2,1)S(1)}, u32[]{:S(2)}, u32[]{:S(2)}) %collective-permute-start.9) | collective-permute-done | bytes 122912 | tf_op jit(solution)/shard_map/ppermute | solution.py:62
  64.9 5.5 %collective-permute-done.10 = bf16[4,1,40,384]{3,2,1,0:T(8,128)(2,1)S(1)} collective-permute-done((bf16[4,1,40,384]{3,2,1,0:T(8,128)(2,1)S(1)}, bf16[4,1,40,384]{3,2,1,0:T(8,128)(2,1)S(1)}, u32[]{:S(2)}, u32[]{:S(2)}) %collective-permute-start.10) | collective-permute-done | bytes 122912 | tf_op jit(solution)/shard_map/ppermute | solution.py:62
  70.4 5.5 %collective-permute-done.11 = bf16[4,1,40,384]{3,2,1,0:T(8,128)(2,1)S(1)} collective-permute-done((bf16[4,1,40,384]{3,2,1,0:T(8,128)(2,1)S(1)}, bf16[4,1,40,384]{3,2,1,0:T(8,128)(2,1)S(1)}, u32[]{:S(2)}, u32[]{:S(2)}) %collective-permute-start.11) | collective-permute-done | bytes 122912 | tf_op jit(solution)/shard_map/ppermute | solution.py:62
  75.9 5.5 %collective-permute-done.12 = bf16[4,1,40,384]{3,2,1,0:T(8,128)(2,1)S(1)} collective-permute-done((bf16[4,1,40,384]{3,2,1,0:T(8,128)(2,1)S(1)}, bf16[4,1,40,384]{3,2,1,0:T(8,128)(2,1)S(1)}, u32[]{:S(2)}, u32[]{:S(2)}) %collective-permute-start.12) | collective-permute-done | bytes 122912 | tf_op jit(solution)/shard_map/ppermute | solution.py:62
  81.4 5.5 %collective-permute-done.13 = bf16[4,1,40,384]{3,2,1,0:T(8,128)(2,1)S(1)} collective-permute-done((bf16[4,1,40,384]{3,2,1,0:T(8,128)(2,1)S(1)}, bf16[4,1,40,384]{3,2,1,0:T(8,128)(2,1)S(1)}, u32[]{:S(2)}, u32[]{:S(2)}) %collective-permute-start.13) | collective-permute-done | bytes 122912 | tf_op jit(solution)/shard_map/ppermute | solution.py:62
  86.9 0.8 dynamic_slice.11
  87.7 4.8 %collective-permute-done.14 = bf16[4,1,40,384]{3,2,1,0:T(8,128)(2,1)S(1)} collective-permute-done((bf16[4,1,40,384]{3,2,1,0:T(8,128)(2,1)S(1)}, bf16[4,1,40,384]{3,2,1,0:T(8,128)(2,1)S(1)}, u32[]{:S(2)}, u32[]{:S(2)}) %collective-permute-start.14) | collective-permute-done | bytes 122912 | tf_op jit(solution)/shard_map/ppermute | solution.py:62
  92.4 1.1 fusion.35
  93.6 4.4 %collective-permute-done.15 = bf16[4,1,40,384]{3,2,1,0:T(8,128)(2,1)S(1)} collective-permute-done((bf16[4,1,40,384]{3,2,1,0:T(8,128)(2,1)S(1)}, bf16[4,1,40,384]{3,2,1,0:T(8,128)(2,1)S(1)}, u32[]{:S(2)}, u32[]{:S(2)}) %collective-permute-start.15) | collective-permute-done | bytes 122912 | tf_op jit(solution)/shard_map/ppermute | solution.py:62
  98.9 0.2 constant_dynamic-slice_fusion
  99.1 2.3 pad_slice_fusion.5
  101.4 1.4 reshape.148
  102.8 1.9 fusion.36
  104.7 4.4 %reshape.150 = f32[2,18,42,3,3,24]{2,1,0,5,4,3:T(8,128)} reshape(f32[1512,216]{0,1:T(8,128)S(1)} %fusion.36) | data formatting | bytes 2612736 | tf_op jit(solution)/shard_map/reshape | solution.py:40
  109.0 2.9 %reshape.151 = bf16[1512,384]{1,0:T(8,128)(2,1)} reshape(bf16[2,18,42,384]{3,2,1,0:T(8,128)(2,1)} %get-tuple-element.9) | data formatting | bytes 2322432 | tf_op jit(solution)/shard_map/reshape | solution.py:35
  112.0 1.9 fusion.37
  113.9 4.3 %reshape.153 = f32[2,18,42,3,3,24]{2,1,0,5,4,3:T(8,128)} reshape(f32[1512,216]{0,1:T(8,128)S(1)} %fusion.37) | data formatting | bytes 2612736 | tf_op jit(solution)/shard_map/reshape | solution.py:40
  118.2 1.3 reshape.154
  119.5 1.9 fusion.38
  121.4 4.3 %reshape.156 = f32[2,18,42,3,3,24]{2,1,0,5,4,3:T(8,128)} reshape(f32[1512,216]{0,1:T(8,128)S(1)} %fusion.38) | data formatting | bytes 2612736 | tf_op jit(solution)/shard_map/reshape | solution.py:40
  125.8 7.0 %fusion.14 = bf16[2,16,40,24]{2,1,0,3:T(8,128)(2,1)S(1)} fusion(f32[2,18,42,3,3,24]{2,1,0,5,4,3:T(8,128)} %reshape.156, f32[2,18,42,3,3,24]{2,1,0,5,4,3:T(8,128)} %reshape.153, f32[2,18,42,3,3,24]{2,1,0,5,4,3:T(8,128)} %reshape.150, f32[24]{0:T(128)S(1)} %dynamic_slice.11), kind=kLoop, calls=%fused_computation.47 | loop fusion | flops 860160 | bytes 3379296 | tf_op jit(solution)/shard_map/convert_element_type | solution.py:66
  132.8 0.2 copy.67
  133.0 0.2 reshape.192
  133.2 17.9 %all_to_all.27 = bf16[16,2,960]{2,1,0:T(2,128)(2,1)S(1)} all-to-all(bf16[16,2,960]{2,1,0:T(2,128)(2,1)S(1)} %reshape.192), channel_id=1, replica_groups=mesh['tm'=32,'rows'=16] {'rows'}, dimensions={0} | all-to-all | bytes 122880 | tf_op jit(solution)/shard_map/all_to_all | solution.py:67
  151.1 0.2 reshape.193
  151.5 0.4 multiply_reduce_fusion
  152.2 4.2 %collective-permute-start.16 = (bf16[2,1,40,384]{3,2,1,0:T(8,128)(2,1)S(1)}, bf16[2,1,40,384]{3,2,1,0:T(8,128)(2,1)S(1)}, u32[]{:S(2)}, u32[]{:S(2)}) collective-permute-start(bf16[2,1,40,384]{3,2,1,0:T(8,128)(2,1)S(1)} %multiply_convert_fusion), channel_id=1, source_target_pairs={{0,16},{16,32},{32,48},{48,64},{64,80},{80,96},{96,112},{112,128},... | collective-permute-start | bytes 184328 | tf_op jit(solution)/shard_map/ppermute | solution.py:10
  156.4 1.1 collective-permute-done.16
  157.5 0.7 maximum_bitcast_fusion
  158.2 0.8 dynamic_slice.12
  159.0 44.9 %all-gather.2.cloned.1.call-done = bf16[4,16,40,384]{3,2,0,1:T(8,128)(2,1)} async-done(((bf16[4,1,40,384]{3,2,0,1:T(8,128)(2,1)}), bf16[4,16,40,384]{3,2,0,1:T(8,128)(2,1)}) %all-gather.2.cloned.1.call-update) | async-done | bytes 1966096 | tf_op jit(solution)/shard_map/all_gather | solution.py:71
  203.9 4.8 %pad_slice_fusion.2 = (bf16[2,18,42,384]{3,2,0,1:T(8,128)(2,1)S(1)}, bf16[2,18,42,384]{3,2,0,1:T(8,128)(2,1)}, bf16[2,18,42,384]{3,2,0,1:T(8,128)(2,1)S(1)}) fusion(bf16[4,16,40,384]{3,2,0,1:T(8,128)(2,1)} %all-gather.2.cloned.1.call-done), kind=kLoop, calls=%fused_computation.2 | loop fusion | bytes 5449728 | tf_op jit(solution)/shard_map/slice | solution.py:31
  208.9 1.4 reshape.157
  210.2 1.9 fusion.39
  212.1 4.4 %reshape.159 = f32[2,18,42,3,3,24]{2,1,0,5,4,3:T(8,128)} reshape(f32[1512,216]{0,1:T(8,128)S(1)} %fusion.39) | data formatting | bytes 2612736 | tf_op jit(solution)/shard_map/reshape | solution.py:40
  216.5 1.5 copy.55
  217.9 1.4 reshape.160
  219.3 1.9 fusion.40
  221.2 4.3 %reshape.162 = f32[2,18,42,3,3,24]{2,1,0,5,4,3:T(8,128)} reshape(f32[1512,216]{0,1:T(8,128)S(1)} %fusion.40) | data formatting | bytes 2612736 | tf_op jit(solution)/shard_map/reshape | solution.py:40
  225.7 0.3 reshape.163
  226.0 0.6 fusion.41
  226.6 4.3 %reshape.165 = f32[2,18,42,3,3,24]{2,1,0,5,4,3:T(8,128)} reshape(f32[1512,216]{0,1:T(8,128)S(1)} %fusion.41) | data formatting | bytes 2612736 | tf_op jit(solution)/shard_map/reshape | solution.py:40
  231.0 7.0 %fusion.1 = f32[2,16,40,24]{2,1,0,3:T(8,128)S(1)} fusion(f32[2,18,42,3,3,24]{2,1,0,5,4,3:T(8,128)} %reshape.165, f32[2,18,42,3,3,24]{2,1,0,5,4,3:T(8,128)} %reshape.162, f32[2,18,42,3,3,24]{2,1,0,5,4,3:T(8,128)} %reshape.159, f32[24]{0:T(128)S(1)} %dynamic_slice.12), kind=kLoop, calls=%fused_computation.8 | loop fusion | flops 829440 | bytes 3440736 | tf_op jit(solution)/shard_map/add | solution.py:49
  238.0 0.2 copy.66
  238.2 0.7 reshape.194
  238.9 13.2 %all_to_all.28 = f32[16,1,1920]{2,1,0:T(1,128)S(1)} all-to-all(f32[16,1,1920]{2,1,0:T(1,128)S(1)} %reshape.194), channel_id=1, replica_groups=mesh['tm'=32,'rows'=16] {'rows'}, dimensions={0} | all-to-all | bytes 245760 | tf_op jit(solution)/shard_map/all_to_all | solution.py:73
  252.1 0.5 broadcast.94
  252.6 0.9 reduce.5
  253.6 0.7 reshape.195
  254.4 0.6 fusion.33
  (63 shorter events, 1.6 us)
Async XLA Ops:
  6.5 197.4 %all-gather.2.cloned.1.call-start = ((), (), s32[]{:S(2)}) async-start(), calls=%async_computation.2 | async-start | bytes 2088960 | tf_op jit(solution)/shard_map/all_gather | solution.py:71
  8.4 5.2 %collective-permute-start = (bf16[2,1,40,384]{3,2,1,0:T(8,128)(2,1)S(1)}, bf16[2,1,40,384]{3,2,1,0:T(8,128)(2,1)S(1)}, u32[]{:S(2)}, u32[]{:S(2)}) collective-permute-start(bf16[2,1,40,384]{3,2,1,0:T(8,128)(2,1)S(1)} %fusion.32), channel_id=1, source_target_pairs={{0,16},{16,32},{32,48},{48,64},{64,80},{80,96},{96,112},{112,128},... | collective-permute-start | bytes 184328 | tf_op jit(solution)/shard_map/ppermute | solution.py:10
  13.7 5.6 %collective-permute-start.1 = (bf16[4,1,40,384]{3,2,1,0:T(8,128)(2,1)S(1)}, bf16[4,1,40,384]{3,2,1,0:T(8,128)(2,1)S(1)}, u32[]{:S(2)}, u32[]{:S(2)}) collective-permute-start(bf16[4,1,40,384]{3,2,1,0:T(8,128)(2,1)S(1)} %pad_maximum_fusion), channel_id=1, source_target_pairs={{0,1},{1,2},{2,3},{3,4},{4,5},{5,6},{6,7},{7,8},{8,9},{9,10},{10,1... | collective-permute-start | bytes 368648 | tf_op jit(solution)/shard_map/ppermute | solution.py:62
  19.3 6.9 %collective-permute-start.2 = (bf16[4,1,40,384]{3,2,1,0:T(8,128)(2,1)S(1)}, bf16[4,1,40,384]{3,2,1,0:T(8,128)(2,1)S(1)}, u32[]{:S(2)}, u32[]{:S(2)}) collective-permute-start(bf16[4,1,40,384]{3,2,1,0:T(8,128)(2,1)S(1)} %collective-permute-done.1), channel_id=1, source_target_pairs={{0,1},{1,2},{2,3},{3,4},{4,5},{5,6},{6,7},{7,8},{8,9},{9,10},{10,1... | collective-permute-start | bytes 368648 | tf_op jit(solution)/shard_map/ppermute | solution.py:62
  26.2 5.5 %collective-permute-start.3 = (bf16[4,1,40,384]{3,2,1,0:T(8,128)(2,1)S(1)}, bf16[4,1,40,384]{3,2,1,0:T(8,128)(2,1)S(1)}, u32[]{:S(2)}, u32[]{:S(2)}) collective-permute-start(bf16[4,1,40,384]{3,2,1,0:T(8,128)(2,1)S(1)} %collective-permute-done.2), channel_id=1, source_target_pairs={{0,1},{1,2},{2,3},{3,4},{4,5},{5,6},{6,7},{7,8},{8,9},{9,10},{10,1... | collective-permute-start | bytes 368648 | tf_op jit(solution)/shard_map/ppermute | solution.py:62
  31.8 5.5 %collective-permute-start.4 = (bf16[4,1,40,384]{3,2,1,0:T(8,128)(2,1)S(1)}, bf16[4,1,40,384]{3,2,1,0:T(8,128)(2,1)S(1)}, u32[]{:S(2)}, u32[]{:S(2)}) collective-permute-start(bf16[4,1,40,384]{3,2,1,0:T(8,128)(2,1)S(1)} %collective-permute-done.3), channel_id=1, source_target_pairs={{0,1},{1,2},{2,3},{3,4},{4,5},{5,6},{6,7},{7,8},{8,9},{9,10},{10,1... | collective-permute-start | bytes 368648 | tf_op jit(solution)/shard_map/ppermute | solution.py:62
  37.3 5.5 %collective-permute-start.5 = (bf16[4,1,40,384]{3,2,1,0:T(8,128)(2,1)S(1)}, bf16[4,1,40,384]{3,2,1,0:T(8,128)(2,1)S(1)}, u32[]{:S(2)}, u32[]{:S(2)}) collective-permute-start(bf16[4,1,40,384]{3,2,1,0:T(8,128)(2,1)S(1)} %collective-permute-done.4), channel_id=1, source_target_pairs={{0,1},{1,2},{2,3},{3,4},{4,5},{5,6},{6,7},{7,8},{8,9},{9,10},{10,1... | collective-permute-start | bytes 368648 | tf_op jit(solution)/shard_map/ppermute | solution.py:62
  42.8 5.5 %collective-permute-start.6 = (bf16[4,1,40,384]{3,2,1,0:T(8,128)(2,1)S(1)}, bf16[4,1,40,384]{3,2,1,0:T(8,128)(2,1)S(1)}, u32[]{:S(2)}, u32[]{:S(2)}) collective-permute-start(bf16[4,1,40,384]{3,2,1,0:T(8,128)(2,1)S(1)} %collective-permute-done.5), channel_id=1, source_target_pairs={{0,1},{1,2},{2,3},{3,4},{4,5},{5,6},{6,7},{7,8},{8,9},{9,10},{10,1... | collective-permute-start | bytes 368648 | tf_op jit(solution)/shard_map/ppermute | solution.py:62
  48.3 5.5 %collective-permute-start.7 = (bf16[4,1,40,384]{3,2,1,0:T(8,128)(2,1)S(1)}, bf16[4,1,40,384]{3,2,1,0:T(8,128)(2,1)S(1)}, u32[]{:S(2)}, u32[]{:S(2)}) collective-permute-start(bf16[4,1,40,384]{3,2,1,0:T(8,128)(2,1)S(1)} %collective-permute-done.6), channel_id=1, source_target_pairs={{0,1},{1,2},{2,3},{3,4},{4,5},{5,6},{6,7},{7,8},{8,9},{9,10},{10,1... | collective-permute-start | bytes 368648 | tf_op jit(solution)/shard_map/ppermute | solution.py:62
  53.8 5.5 %collective-permute-start.8 = (bf16[4,1,40,384]{3,2,1,0:T(8,128)(2,1)S(1)}, bf16[4,1,40,384]{3,2,1,0:T(8,128)(2,1)S(1)}, u32[]{:S(2)}, u32[]{:S(2)}) collective-permute-start(bf16[4,1,40,384]{3,2,1,0:T(8,128)(2,1)S(1)} %collective-permute-done.7), channel_id=1, source_target_pairs={{0,1},{1,2},{2,3},{3,4},{4,5},{5,6},{6,7},{7,8},{8,9},{9,10},{10,1... | collective-permute-start | bytes 368648 | tf_op jit(solution)/shard_map/ppermute | solution.py:62
  59.3 5.5 %collective-permute-start.9 = (bf16[4,1,40,384]{3,2,1,0:T(8,128)(2,1)S(1)}, bf16[4,1,40,384]{3,2,1,0:T(8,128)(2,1)S(1)}, u32[]{:S(2)}, u32[]{:S(2)}) collective-permute-start(bf16[4,1,40,384]{3,2,1,0:T(8,128)(2,1)S(1)} %collective-permute-done.8), channel_id=1, source_target_pairs={{0,1},{1,2},{2,3},{3,4},{4,5},{5,6},{6,7},{7,8},{8,9},{9,10},{10,1... | collective-permute-start | bytes 368648 | tf_op jit(solution)/shard_map/ppermute | solution.py:62
  64.9 5.5 %collective-permute-start.10 = (bf16[4,1,40,384]{3,2,1,0:T(8,128)(2,1)S(1)}, bf16[4,1,40,384]{3,2,1,0:T(8,128)(2,1)S(1)}, u32[]{:S(2)}, u32[]{:S(2)}) collective-permute-start(bf16[4,1,40,384]{3,2,1,0:T(8,128)(2,1)S(1)} %collective-permute-done.9), channel_id=1, source_target_pairs={{0,1},{1,2},{2,3},{3,4},{4,5},{5,6},{6,7},{7,8},{8,9},{9,10},{10,1... | collective-permute-start | bytes 368648 | tf_op jit(solution)/shard_map/ppermute | solution.py:62
  70.4 5.5 %collective-permute-start.11 = (bf16[4,1,40,384]{3,2,1,0:T(8,128)(2,1)S(1)}, bf16[4,1,40,384]{3,2,1,0:T(8,128)(2,1)S(1)}, u32[]{:S(2)}, u32[]{:S(2)}) collective-permute-start(bf16[4,1,40,384]{3,2,1,0:T(8,128)(2,1)S(1)} %collective-permute-done.10), channel_id=1, source_target_pairs={{0,1},{1,2},{2,3},{3,4},{4,5},{5,6},{6,7},{7,8},{8,9},{9,10},{10,1... | collective-permute-start | bytes 368648 | tf_op jit(solution)/shard_map/ppermute | solution.py:62
  75.9 5.5 %collective-permute-start.12 = (bf16[4,1,40,384]{3,2,1,0:T(8,128)(2,1)S(1)}, bf16[4,1,40,384]{3,2,1,0:T(8,128)(2,1)S(1)}, u32[]{:S(2)}, u32[]{:S(2)}) collective-permute-start(bf16[4,1,40,384]{3,2,1,0:T(8,128)(2,1)S(1)} %collective-permute-done.11), channel_id=1, source_target_pairs={{0,1},{1,2},{2,3},{3,4},{4,5},{5,6},{6,7},{7,8},{8,9},{9,10},{10,1... | collective-permute-start | bytes 368648 | tf_op jit(solution)/shard_map/ppermute | solution.py:62
  81.4 5.5 %collective-permute-start.13 = (bf16[4,1,40,384]{3,2,1,0:T(8,128)(2,1)S(1)}, bf16[4,1,40,384]{3,2,1,0:T(8,128)(2,1)S(1)}, u32[]{:S(2)}, u32[]{:S(2)}) collective-permute-start(bf16[4,1,40,384]{3,2,1,0:T(8,128)(2,1)S(1)} %collective-permute-done.12), channel_id=1, source_target_pairs={{0,1},{1,2},{2,3},{3,4},{4,5},{5,6},{6,7},{7,8},{8,9},{9,10},{10,1... | collective-permute-start | bytes 368648 | tf_op jit(solution)/shard_map/ppermute | solution.py:62
  86.9 5.5 %collective-permute-start.14 = (bf16[4,1,40,384]{3,2,1,0:T(8,128)(2,1)S(1)}, bf16[4,1,40,384]{3,2,1,0:T(8,128)(2,1)S(1)}, u32[]{:S(2)}, u32[]{:S(2)}) collective-permute-start(bf16[4,1,40,384]{3,2,1,0:T(8,128)(2,1)S(1)} %collective-permute-done.13), channel_id=1, source_target_pairs={{0,1},{1,2},{2,3},{3,4},{4,5},{5,6},{6,7},{7,8},{8,9},{9,10},{10,1... | collective-permute-start | bytes 368648 | tf_op jit(solution)/shard_map/ppermute | solution.py:62
  92.4 5.5 %collective-permute-start.15 = (bf16[4,1,40,384]{3,2,1,0:T(8,128)(2,1)S(1)}, bf16[4,1,40,384]{3,2,1,0:T(8,128)(2,1)S(1)}, u32[]{:S(2)}, u32[]{:S(2)}) collective-permute-start(bf16[4,1,40,384]{3,2,1,0:T(8,128)(2,1)S(1)} %collective-permute-done.14), channel_id=1, source_target_pairs={{0,1},{1,2},{2,3},{3,4},{4,5},{5,6},{6,7},{7,8},{8,9},{9,10},{10,1... | collective-permute-start | bytes 368648 | tf_op jit(solution)/shard_map/ppermute | solution.py:62
  125.8 26.3 %copy-start.2 = (f32[384]{0:T(512)S(1)}, f32[384]{0:T(512)}, u32[]{:S(2)}) copy-start(f32[384]{0:T(512)} %param.11) | copy-start | bytes 4612
  125.8 33.1 %copy-start.1 = (bf16[24,3,3,3,384]{4,0,3,2,1:T(8,128)(2,1)S(1)}, bf16[24,3,3,3,384]{4,0,3,2,1:T(8,128)(2,1)}, u32[]{:S(2)}) copy-start(bf16[24,3,3,3,384]{4,0,3,2,1:T(8,128)(2,1)} %param.12) | copy-start | bytes 1492996
  152.2 5.3 %collective-permute-start.16 = (bf16[2,1,40,384]{3,2,1,0:T(8,128)(2,1)S(1)}, bf16[2,1,40,384]{3,2,1,0:T(8,128)(2,1)S(1)}, u32[]{:S(2)}, u32[]{:S(2)}) collective-permute-start(bf16[2,1,40,384]{3,2,1,0:T(8,128)(2,1)S(1)} %multiply_convert_fusion), channel_id=1, source_target_pairs={{0,16},{16,32},{32,48},{48,64},{64,80},{80,96},{96,112},{112,128},... | collective-permute-start | bytes 184328 | tf_op jit(solution)/shard_map/ppermute | solution.py:10
  231.0 23.5 %copy-start = (bf16[2,1,40,384]{3,2,1,0:T(8,128)(2,1)S(1)}, bf16[2,1,40,384]{3,2,1,0:T(8,128)(2,1)}, u32[]{:S(2)}) copy-start(bf16[2,1,40,384]{3,2,1,0:T(8,128)(2,1)} %param.7) | copy-start | bytes 184324
Sparse Core Ops, SparseCore 0:
  158.3 45.5 all-gather.1
